TPU v7x, 32 devices: a whole 2x2x4 slice. The times are simulated.
32 devices in a mesh: groups: 2 (over y), seq: 4 (over x, core), fsdp: 4 (over z).
Axes of the slice: x: 2, y: 2, z: 4, core: 2. Of those that a mesh axis runs over, the one named last changes fastest.
Arguments:
- tokens: bfloat16 [16, 512, 1536], P(('groups', 'fsdp'), 'seq'), parts along dimension 0, may hold values from -6 to 6
- in_weight: bfloat16 [1536, 4608], P(None, 'fsdp'), may hold values from -0.15625 to 0.15625
- short_weight: float32 [3, 4608], replicated, may hold values from -3.5 to 3.5
- basis_in: float32 [17, 64], replicated, may hold values from -4 to 4
- basis_bias: float32 [64], replicated, may hold values from -3.140625 to 3.140625
- basis_mid: float32 [64, 64], replicated, may hold values from -1.5 to 1.5
- basis_shift: float32 [64], replicated, may hold values from -3.140625 to 3.140625
- response_out: float32 [2, 64, 1536], P(None, None, 'fsdp'), may hold values from -0.0234375 to 0.0234375
- skip_gain: float32 [1536], P('fsdp'), may hold values from -4 to 4
- block_counts: int32 [16, 4], P(('groups', 'fsdp'), 'seq'), parts along dimension 0, may hold values from 1 to 128, as said below
Outputs:
- mixed: bfloat16 [16, 512, 1536], P(('groups', 'fsdp'), 'seq'), parts along dimension 0
There are 2 independent parts, one for each index of `groups`. A program takes and returns all parts, laid end to end along the dimension named above; an argument that names none is the same for every part. Nothing has to cross between parts.
Inputs may be any that keep to these rules, and one draw needn't show every extreme that they name: `block_counts`: in every table one block holds all 128 tokens and another holds a single token.
All inputs are finite; a program needn't handle non-finite values.
Results may differ from a plain program's by a relative error of at most 0.007.
Values may be sent and summed in bfloat16 or wider, within the bound.
No kernel may reach another device: no remote copies, remote signals or barrier semaphores. Data moves between devices by JAX's collectives and lax.ppermute only.
A program may use at most 128 MiB of HBM per device.

v0:
```python
import jax
import jax.numpy as jnp
from jax import lax
from jax.sharding import PartitionSpec as P


def padded_2(cells, sides, width):
    for axis, dim in sides:
        count = lax.axis_size(axis)
        ends = count - 1
        head = lax.slice_in_dim(cells, 0, width, axis=dim)
        tail = lax.slice_in_dim(cells, cells.shape[dim] - width, cells.shape[dim], axis=dim)
        cells = jnp.concatenate(
            [
                lax.ppermute(tail, axis, [(i, (i + 1) % count) for i in range(ends)]),
                cells,
                lax.ppermute(head, axis, [((i + 1) % count, i) for i in range(ends)]),
            ],
            axis=dim,
        )
    return cells


def filter_basis(lag_values, total_len, basis_in, basis_bias, basis_mid, basis_shift):
    band_count = (basis_in.shape[0] - 1) // 2
    distance = jnp.abs(lag_values)
    periods = (2 ** (jnp.arange(band_count, dtype=jnp.int32) + 2) + 1).astype(jnp.int32)
    angles = (
        2.0
        * jnp.pi
        * (distance[:, None] % periods[None, :]).astype(jnp.float32)
        / periods[None, :].astype(jnp.float32)
    )
    linear = distance.astype(jnp.float32)[:, None] / total_len
    encoded = jnp.concatenate([linear, jnp.cos(angles), jnp.sin(angles)], axis=1)
    hidden = jnp.sin(jnp.dot(encoded, basis_in, precision=lax.Precision.HIGHEST) + basis_bias)
    return jnp.sin(jnp.dot(hidden, basis_mid, precision=lax.Precision.HIGHEST) + basis_shift)


def forward_table(block_len):
    period = 2 * block_len
    frequency = jnp.arange(block_len, dtype=jnp.int32)[:, None]
    samples = jnp.arange(period, dtype=jnp.int32)[None, :]
    phases = 2.0 * jnp.pi / period * (frequency * samples % period).astype(jnp.float32)
    alternate = (1 - 2 * (samples % 2)).astype(jnp.float32)
    real_rows = jnp.cos(phases)
    imag_rows = jnp.where(frequency == 0, alternate, -jnp.sin(phases))
    return jnp.concatenate([real_rows, imag_rows], axis=0)


def inverse_table(block_len):
    period = 2 * block_len
    places = jnp.arange(block_len, dtype=jnp.int32)[:, None]
    frequency = jnp.arange(block_len, dtype=jnp.int32)[None, :]
    phases = 2.0 * jnp.pi / period * (places * frequency % period).astype(jnp.float32)
    alternate = (1 - 2 * (places % 2)).astype(jnp.float32)
    real_cols = jnp.where(frequency == 0, 1.0, 2.0 * jnp.cos(phases)) / period
    imag_cols = jnp.where(frequency == 0, alternate, -2.0 * jnp.sin(phases)) / period
    return jnp.concatenate([real_cols, imag_cols], axis=1)


def packed_product(response, signal, block_len):
    first_slot = (jnp.arange(block_len) == 0)[:, None]
    resp_real = response[..., :block_len, :]
    resp_imag = response[..., block_len:, :]
    sig_real = signal[..., :block_len, :]
    sig_imag = signal[..., block_len:, :]
    cross_term = resp_imag * sig_imag
    prod_real = resp_real * sig_real - jnp.where(first_slot, 0.0, cross_term)
    prod_imag = jnp.where(first_slot, cross_term, resp_real * sig_imag + resp_imag * sig_real)
    return jnp.concatenate([prod_real, prod_imag], axis=-2)


def shards(
    tokens,
    in_weight,
    short_weight,
    basis_in,
    basis_bias,
    basis_mid,
    basis_shift,
    response_out,
    skip_gain,
    block_counts,
):
    seq_dev, block_len, width = tokens.shape
    group_tokens = lax.all_gather(tokens, "fsdp", axis=0, tiled=True)
    group_rows = group_tokens.shape[0]
    local_cols = in_weight.shape[1]
    partial = jnp.dot(
        group_tokens.reshape(group_rows * block_len, width),
        in_weight,
        preferred_element_type=jnp.float32,
    ).astype(jnp.bfloat16)
    partial = partial.reshape(group_rows, block_len, local_cols)
    projected = lax.all_to_all(partial, "fsdp", 0, 2, tiled=True)
    padded = padded_2(projected, (("seq", 1),), 1)
    shorted = (
        short_weight[0] * padded[:, :-2]
        + short_weight[1] * padded[:, 1:-1]
        + short_weight[2] * padded[:, 2:]
    )
    query_gate = shorted[:, :, :width]
    key_part = shorted[:, :, width : 2 * width]
    value_part = shorted[:, :, 2 * width :]
    valid_mask = (jnp.arange(block_len, dtype=jnp.int32)[None, :] < block_counts).astype(
        jnp.float32
    )
    carried = (key_part * value_part * valid_mask[:, :, None]).astype(jnp.bfloat16)
    full_out, full_skip = (
        lax.all_gather(response_out, "fsdp", axis=2, tiled=True),
        lax.all_gather(skip_gain, "fsdp", axis=0, tiled=True),
    )
    stacked_out = full_out.reshape(2 * full_out.shape[1], width)
    seq_count = lax.axis_size("seq")
    position = lax.axis_index("seq")
    total_len = float(seq_count * block_len)
    forward = forward_table(block_len)
    forward_half = forward[:, :block_len]
    inverse = inverse_table(block_len)
    circular = jnp.arange(2 * block_len, dtype=jnp.int32)
    wrapped = jnp.where(circular < block_len, circular, circular - 2 * block_len)

    def kernel_response(offset, out_cols):
        lag_values = offset + wrapped
        basis_rows = filter_basis(
            lag_values, total_len, basis_in, basis_bias, basis_mid, basis_shift
        )
        ahead_mask = (lag_values >= 0).astype(jnp.float32)[:, None]
        paired = jnp.concatenate([basis_rows * ahead_mask, basis_rows * (1.0 - ahead_mask)], axis=1)
        return jnp.dot(
            jnp.dot(forward, paired, precision=lax.Precision.HIGHEST),
            out_cols,
            precision=lax.Precision.HIGHEST,
        )

    def add_block(spectrum, block_rows, start):
        offset = position * block_len - start
        response = kernel_response(offset, stacked_out)
        signal = jnp.einsum(
            "fc,scd->sfd",
            forward_half,
            block_rows.astype(jnp.float32),
            precision=lax.Precision.HIGHEST,
        )
        return spectrum + packed_product(response[None], signal, block_len)

    initial = jnp.zeros((seq_dev, 2 * block_len, width), jnp.float32)
    piece = lax.all_gather(carried, "seq", axis=1, tiled=True)
    piece_rows = piece.shape[1]
    block_total = piece_rows // block_len

    def one_block(block_index, carry):
        block_rows = lax.dynamic_slice_in_dim(piece, block_index * block_len, block_len, 1)
        return add_block(carry, block_rows, block_index * block_len)

    spectrum = lax.fori_loop(0, block_total, one_block, initial)
    conv = jnp.einsum("if,sfd->sid", inverse, spectrum, precision=lax.Precision.HIGHEST)
    return (query_gate * (conv + full_skip * carried.astype(jnp.float32))).astype(jnp.bfloat16)


def solution(mesh):
    placed = (
        P(("groups", "fsdp"), "seq", None),
        P(None, "fsdp"),
        P(),
        P(),
        P(),
        P(),
        P(),
        P(None, None, "fsdp"),
        P("fsdp"),
        P(("groups", "fsdp"), "seq"),
    )
    return jax.shard_map(
        shards,
        mesh=mesh,
        in_specs=placed,
        out_specs=P(("groups", "fsdp"), "seq", None),
        check_vma=False,
    )
```

profile of v0, /device:TPU:2, one launch (start us, length us, event | category | flops | bytes accessed | tf_op | source)
XLA Modules:
  0.0 302.2 jit_solution(2501134679842409714)
XLA Ops:
  7.3 66.4 %all-gather.4.cloned.1.call-done = bf16[8,128,1536]{2,1,0:T(8,128)(2,1)} async-done(((bf16[2,128,1536]{2,1,0:T(8,128)(2,1)}), bf16[8,128,1536]{2,1,0:T(8,128)(2,1)}) %all-gather.4.cloned.1.call-update) | async-done | bytes 3145744 | tf_op jit(solution)/shard_map/all_gather | solution.py:87
  73.7 7.6 %convolution_convert_fusion = bf16[1024,1152]{1,0:T(8,128)(2,1)} fusion(bf16[1024,1536]{1,0:T(8,128)(2,1)} %bitcast.65, bf16[1536,1152]{1,0:T(8,128)(2,1)S(1)} %copy-done), kind=kOutput, calls=%fused_computation.58 | convolution fusion | flops 3625058304 | bytes 9043968 | tf_op jit(solution)/shard_map/dot_general | solution.py:90
  81.3 4.6 %all-to-all-start = ((bf16[8,128,1152]{2,1,0:T(8,128)(2,1)}), bf16[8,128,1152]{2,1,0:T(8,128)(2,1)}, u32[]{:S(2)}, u32[]{:S(2)}) async-start(bf16[8,128,1152]{2,1,0:T(8,128)(2,1)} %bitcast.63), calls=%async_computation | async-start | bytes 4718592 | tf_op jit(solution)/shard_map/all_to_all | solution.py:96
  86.0 54.0 %all-to-all-done = bf16[8,128,1152]{2,1,0:T(8,128)(2,1)} async-done(((bf16[8,128,1152]{2,1,0:T(8,128)(2,1)}), bf16[8,128,1152]{2,1,0:T(8,128)(2,1)}, u32[]{:S(2)}, u32[]{:S(2)}) %all-to-all-start) | async-done | bytes 2359328 | tf_op jit(solution)/shard_map/all_to_all | solution.py:96
  140.0 4.3 %copy.20 = bf16[4,2,128,1152]{2,3,0,1:T(8,128)(2,1)} copy(bf16[4,2,128,1152]{3,2,1,0:T(8,128)(2,1)} %bitcast.2) | data formatting | bytes 4718592 | tf_op jit(solution)/shard_map/all_to_all | solution.py:96
  144.3 5.3 %fusion.56 = (bf16[2,1,4608]{1,2,0:T(8,128)(2,1)}, bf16[2,1,4608]{1,2,0:T(8,128)(2,1)}) fusion(bf16[2,128,4608]{1,2,0:T(8,128)(2,1)} %bitcast.60), kind=kLoop, calls=%fused_computation.111 | loop fusion | bytes 73728 | tf_op jit(solution)/shard_map/slice | solution.py:12
  149.6 2.7 copy.21
  154.2 2.7 copy.23
  156.9 3.6 %collective-permute-start.1 = (bf16[2,1,4608]{2,0,1:T(2,128)(2,1)}, bf16[2,1,4608]{2,0,1:T(2,128)(2,1)}, u32[]{:S(2)}, u32[]{:S(2)}) collective-permute-start(bf16[2,1,4608]{2,0,1:T(2,128)(2,1)} %copy.23), channel_id=1, source_target_pairs={{4,0},{8,4},{12,8},{5,1},{9,5},{13,9},{6,2},{10,6},{14,10},{7,3},{... | collective-permute-start | bytes 55304 | tf_op jit(solution)/shard_map/ppermute | solution.py:17
  162.3 2.6 copy.22
  164.9 2.6 copy.24
  167.6 7.7 %multiply_add_fusion = f32[2,128,4608]{1,2,0:T(8,128)S(1)} fusion(bf16[2,128,4608]{1,2,0:T(8,128)(2,1)} %bitcast.61, bf16[2,1,4608]{1,2,0:T(8,128)(2,1)} %copy.24, bf16[2,1,4608]{1,2,0:T(8,128)(2,1)} %copy.22, f32[4608]{0:T(1024)} %get-tuple-element.353, f32[4608]{0:T(1024)} %get-tuple-element.354, f32[4608]{0:T(1024)} %get-tuple-element.352), kind=kLoop, calls=%fused_computation.57 | loop fusion | flops 16515072 | bytes 7170048 | tf_op jit(solution)/shard_map/add | solution.py:99
  178.5 11.9 %all-gather = f32[4,1,384]{2,1,0:T(1,128)S(1)} all-gather(f32[1,1,384]{2,1,0:T(1,128)S(1)} %reshape.183), channel_id=1, replica_groups=mesh['groups'=2,'seq'=4,'fsdp'=4] {'fsdp'}, dimensions={0}, use_global_device_ids=true | all-gather | bytes 7680 | tf_op jit(solution)/shard_map/all_gather | solution.py:112
  193.3 18.5 %all_gather.13 = f32[2,64,1536]{2,1,0:T(8,128)} all-gather(f32[2,64,384]{2,1,0:T(8,128)} %param.19), channel_id=1, replica_groups=mesh['groups'=2,'seq'=4,'fsdp'=4] {'fsdp'}, dimensions={2}, use_global_device_ids=true | all-gather | bytes 983040 | tf_op jit(solution)/shard_map/all_gather | solution.py:111
  211.8 72.5 %while.16 = (s32[]{:T(128)}, f32[2,256,1536]{2,1,0:T(8,128)}, s32[]{:T(128)}, f32[17,64]{1,0:T(8,128)}, f32[64]{0:T(128)}, /*index=5*/f32[64,64]{1,0:T(8,128)}, ...) while((s32[]{:T(128)}, f32[2,256,1536]{2,1,0:T(8,128)}, ...), condition=%wide.region_1.2_spmd.clone, body=%wide.region_0.1_spmd.clone.sunk | while | flops 1934166400 | bytes 34141608 | solution.py:157
  216.0 2.6 convolution_bitcast_fusion.6
  219.8 2.7 convolution_bitcast_fusion.5
  222.5 2.5 select_subtract_fusion.2
  225.0 4.3 %maximum_add_fusion.2 = f32[2,256,1536]{2,1,0:T(8,128)} fusion(f32[2,128,1536]{2,1,0:T(8,128)} %get-tuple-element.484, f32[2,128,1536]{2,1,0:T(8,128)} %get-tuple-element.485, f32[2,256,1536]{2,1,0:T(8,128)} %get-tuple-element.502, pred[]{:T(512)S(6)} %compare.7), kind=kLoop, calls=%fused_computation.2.clone.1 | loop fusion | flops 2359296 | bytes 9437185 | tf_op jit(solution)/shard_map/while/body/eval_jaxpr/add | solution.py:146
  233.4 2.6 convolution_bitcast_fusion.6
  237.2 2.7 convolution_bitcast_fusion.5
  239.9 2.5 select_subtract_fusion.2
  242.4 5.2 %maximum_add_fusion.2 = f32[2,256,1536]{2,1,0:T(8,128)} fusion(f32[2,128,1536]{2,1,0:T(8,128)} %get-tuple-element.484, f32[2,128,1536]{2,1,0:T(8,128)} %get-tuple-element.485, f32[2,256,1536]{2,1,0:T(8,128)} %get-tuple-element.502, pred[]{:T(512)S(6)} %compare.7), kind=kLoop, calls=%fused_computation.2.clone.1 | loop fusion | flops 2359296 | bytes 9437185 | tf_op jit(solution)/shard_map/while/body/eval_jaxpr/add | solution.py:146
  251.7 2.6 convolution_bitcast_fusion.6
  255.6 2.7 convolution_bitcast_fusion.5
  258.3 2.5 select_subtract_fusion.2
  260.7 5.2 %maximum_add_fusion.2 = f32[2,256,1536]{2,1,0:T(8,128)} fusion(f32[2,128,1536]{2,1,0:T(8,128)} %get-tuple-element.484, f32[2,128,1536]{2,1,0:T(8,128)} %get-tuple-element.485, f32[2,256,1536]{2,1,0:T(8,128)} %get-tuple-element.502, pred[]{:T(512)S(6)} %compare.7), kind=kLoop, calls=%fused_computation.2.clone.1 | loop fusion | flops 2359296 | bytes 9437185 | tf_op jit(solution)/shard_map/while/body/eval_jaxpr/add | solution.py:146
  270.1 2.6 convolution_bitcast_fusion.6
  273.9 2.7 convolution_bitcast_fusion.5
  276.6 2.5 select_subtract_fusion.2
  279.1 5.2 %maximum_add_fusion.2 = f32[2,256,1536]{2,1,0:T(8,128)} fusion(f32[2,128,1536]{2,1,0:T(8,128)} %get-tuple-element.484, f32[2,128,1536]{2,1,0:T(8,128)} %get-tuple-element.485, f32[2,256,1536]{2,1,0:T(8,128)} %get-tuple-element.502, pred[]{:T(512)S(6)} %compare.7), kind=kLoop, calls=%fused_computation.2.clone.1 | loop fusion | flops 2359296 | bytes 9437185 | tf_op jit(solution)/shard_map/while/body/eval_jaxpr/add | solution.py:146
  284.3 8.8 %fusion.32 = bf16[2,128,1536]{1,2,0:T(8,128)(2,1)} fusion(f32[2,128,4608]{1,2,0:T(8,128)} %copy-done.3, f32[2,256,1536]{2,1,0:T(8,128)} %get-tuple-element.280, bf16[2,128,1536]{1,2,0:T(8,128)(2,1)} %fusion.31, f32[1536]{0:T(1024)S(1)} %reshape.184, f32[128,128]{1,0:T(8,128)} %get-tuple-element.392, f32[128,128]{1,0:T(8,128)} %get-tuple-element.391), kind=kOutput, calls=%fused_computation.67 | convolution fusion | flops 1209958400 | bytes 6428672 | tf_op jit(solution)/shard_map/if,sfd->sid/dot_general | solution.py:158
  (91 shorter events, 34.3 us)
Async XLA Ops:
  6.5 67.2 %copy-start = (bf16[1536,1152]{1,0:T(8,128)(2,1)S(1)}, bf16[1536,1152]{1,0:T(8,128)(2,1)}, u32[]{:S(2)}) copy-start(bf16[1536,1152]{1,0:T(8,128)(2,1)} %param.13) | copy-start | bytes 10616836
  6.5 67.2 %all-gather.4.cloned.1.call-start = ((), (), s32[]{:S(2)}) async-start(), calls=%async_computation.1 | async-start | bytes 3932160 | tf_op jit(solution)/shard_map/all_gather | solution.py:87
  81.3 4.7 %copy-start.5 = (s32[2,1]{0,1:T(1,128)S(1)}, s32[2,1]{0,1:T(1,128)}, u32[]{:S(2)}) copy-start(s32[2,1]{0,1:T(1,128)} %param.21) | copy-start | bytes 28
  81.3 58.8 %all-to-all-start = ((bf16[8,128,1152]{2,1,0:T(8,128)(2,1)}), bf16[8,128,1152]{2,1,0:T(8,128)(2,1)}, u32[]{:S(2)}, u32[]{:S(2)}) async-start(bf16[8,128,1152]{2,1,0:T(8,128)(2,1)} %bitcast.63), calls=%async_computation | async-start | bytes 4718592 | tf_op jit(solution)/shard_map/all_to_all | solution.py:96
  85.9 125.9 %all-gather.6.cloned.1.call-start = ((), (), s32[]{:S(2)}) async-start(), calls=%async_computation.2 | async-start | bytes 3932160 | tf_op jit(solution)/shard_map/all_gather | solution.py:149
  152.3 10.0 %collective-permute-start = (bf16[2,1,4608]{2,0,1:T(2,128)(2,1)}, bf16[2,1,4608]{2,0,1:T(2,128)(2,1)}, u32[]{:S(2)}, u32[]{:S(2)}) collective-permute-start(bf16[2,1,4608]{2,0,1:T(2,128)(2,1)} %copy.21), channel_id=1, source_target_pairs={{0,4},{4,8},{8,12},{1,5},{5,9},{9,13},{2,6},{6,10},{10,14},{3,7},{... | collective-permute-start | bytes 55304 | tf_op jit(solution)/shard_map/ppermute | solution.py:15
  156.9 8.0 %collective-permute-start.1 = (bf16[2,1,4608]{2,0,1:T(2,128)(2,1)}, bf16[2,1,4608]{2,0,1:T(2,128)(2,1)}, u32[]{:S(2)}, u32[]{:S(2)}) collective-permute-start(bf16[2,1,4608]{2,0,1:T(2,128)(2,1)} %copy.23), channel_id=1, source_target_pairs={{4,0},{8,4},{12,8},{5,1},{9,5},{13,9},{6,2},{10,6},{14,10},{7,3},{... | collective-permute-start | bytes 55304 | tf_op jit(solution)/shard_map/ppermute | solution.py:17
  175.2 2.1 copy-start.3
  177.4 1.1 copy-start.4
  219.8 2.7 copy-start.1
  219.8 2.7 copy-start.2
  237.2 2.7 copy-start.1
  237.2 2.7 copy-start.2
  255.6 2.7 copy-start.1
  255.6 2.7 copy-start.2
  273.9 2.7 copy-start.1
  273.9 2.7 copy-start.2
Sparse Core Ops, SparseCore 0:
  8.9 64.7 all-gather.3
  178.6 26.8 all-gather.5
where the time goes:
time: 304 us; the launch traced here: 302 us
  waiting for transfers between devices  121 us (40%)
  matrix products  52.3 us (17%)
  other arithmetic  42.7 us (14%)
  local copies, waits for them, and re-layouts  31.5 us (10%)
  blocking collectives  30.4 us (10%)
  between operations  13.5 us (4%)
  starting transfers between devices  10.2 us (3%)
    all_gather x1, waiting for transfers between devices, shards(): group_tokens = lax.all_gather(tokens, 'fsdp', axis=0, tiled=True)  66.4 us
    all_to_all x1, waiting for transfers between devices, shards(): projected = lax.all_to_all(partial, 'fsdp', 0, 2, tiled=True)  54 us
    add x4, other arithmetic, add_block(): return spectrum + packed_product(response[None], signal, block_len)  19.9 us
    all_gather x1, blocking collectives, shards(): lax.all_gather(response_out, 'fsdp', axis=2, tiled=True)  18.5 us
    all_gather x1, blocking collectives, shards(): lax.all_gather(skip_gain, 'fsdp', axis=0, tiled=True)  11.9 us
    dot_general x4, matrix products, add_block(): jnp.einsum('fc,scd->sfd', forward_half, block_rows.astype(jnp.float32), p...  10.7 us
    dot_general x4, matrix products, kernel_response(): jnp.dot(jnp.dot(forward, paired, precision=lax.Precision.HIGHEST), out_co...  10.3 us
    sub x4, other arithmetic, packed_product(): prod_real = resp_real * sig_real - jnp.where(first_slot, 0.0, cross_term)  9.89 us
  transfers between devices with their start and end apart: 5, of which 2 were waited for; matrix products, arithmetic and copies ran while one was open for 3% of the time, Pallas kernels for 0%

commit v1 on v0

--- a/solution.py
+++ b/solution.py
@@ -2,6 +2,20 @@
 import jax.numpy as jnp
 from jax import lax
 from jax.sharding import PartitionSpec as P
+from jax.lax import axis_index, axis_size, ppermute
+
+
+def draft_scenes(incoming_x, axis_id):
+    n_parts = axis_size(axis_id)
+    t1 = sorted(((it, (it + 1) % n_parts) for it in range(n_parts)))
+    value_now = incoming_x
+    block_list = [value_now]
+    for idx in range(1, n_parts):
+        value_now = ppermute(value_now, axis_id, t1)
+        block_list.insert(0, value_now)
+    z = jnp.concatenate(block_list, 0)
+    inter = axis_index(axis_id) + 1
+    return jnp.roll(z, inter * incoming_x.shape[0], 0)
 
 
 def padded_2(cells, sides, width):
@@ -84,7 +98,7 @@
     block_counts,
 ):
     seq_dev, block_len, width = tokens.shape
-    group_tokens = lax.all_gather(tokens, "fsdp", axis=0, tiled=True)
+    group_tokens = draft_scenes(tokens, "fsdp")
     group_rows = group_tokens.shape[0]
     local_cols = in_weight.shape[1]
     partial = jnp.dot(

time: 304 us -> 300 us (0.987)
  waiting for transfers between devices: 121 us -> 111 us
  local copies, waits for them, and re-layouts: 31.5 us -> 37.7 us
    all_gather x1 -> x0, waiting for transfers between devices: 66.4 us -> none  [shards(): group_tokens = lax.all_gather(tokens, 'fsdp', axis=0, tiled=True)]
    ppermute x0 -> x3, waiting for transfers between devices: none -> 59.8 us  [draft_scenes(): value_now = ppermute(value_now, axis_id, t1)]
    unnamed x10 -> x23, local copies, waits for them, and re-layouts: 2.14 us -> 7.95 us
  transfers between devices with their start and end apart: 5 -> 7, of which waited for: 2 -> 4; matrix products, arithmetic and copies ran while one was open for 3% -> 3% of each run, Pallas kernels for 0% -> 0%
where the time goes in v1:
time: 300 us; the launch traced here: 298 us
  waiting for transfers between devices  111 us (37%)
  matrix products  50.2 us (17%)
  other arithmetic  42.8 us (14%)
  local copies, waits for them, and re-layouts  37.7 us (13%)
  blocking collectives  30.4 us (10%)
  between operations  13.6 us (5%)
  starting transfers between devices  11.8 us (4%)
    ppermute x3, waiting for transfers between devices, draft_scenes(): value_now = ppermute(value_now, axis_id, t1)  59.8 us
    all_to_all x1, waiting for transfers between devices, shards(): projected = lax.all_to_all(partial, 'fsdp', 0, 2, tiled=True)  51.4 us
    add x4, other arithmetic, add_block(): return spectrum + packed_product(response[None], signal, block_len)  20 us
    all_gather x1, blocking collectives, shards(): lax.all_gather(response_out, 'fsdp', axis=2, tiled=True)  18.5 us
    all_gather x1, blocking collectives, shards(): lax.all_gather(skip_gain, 'fsdp', axis=0, tiled=True)  11.9 us
    dot_general x4, matrix products, add_block(): jnp.einsum('fc,scd->sfd', forward_half, block_rows.astype(jnp.float32), p...  10.7 us
    dot_general x4, matrix products, kernel_response(): jnp.dot(jnp.dot(forward, paired, precision=lax.Precision.HIGHEST), out_co...  10.3 us
    sub x4, other arithmetic, packed_product(): prod_real = resp_real * sig_real - jnp.where(first_slot, 0.0, cross_term)  9.95 us
  transfers between devices with their start and end apart: 7, of which 4 were waited for; matrix products, arithmetic and copies ran while one was open for 3% of the time, Pallas kernels for 0%

profile of v1, /device:TPU:2, one launch (start us, length us, event | category | flops | bytes accessed | tf_op | source)
XLA Modules:
  0.0 298.0 jit_solution(15228415627406417067)
XLA Ops:
  8.1 19.8 %collective-permute-done = bf16[2,128,1536]{2,1,0:T(8,128)(2,1)S(1)} collective-permute-done((bf16[2,128,1536]{2,1,0:T(8,128)(2,1)}, bf16[2,128,1536]{2,1,0:T(8,128)(2,1)S(1)}, u32[]{:S(2)}, u32[]{:S(2)}) %collective-permute-start) | collective-permute-done | bytes 786464 | tf_op jit(solution)/shard_map/ppermute | solution.py:14
  28.8 20.4 %collective-permute-done.1 = bf16[2,128,1536]{2,1,0:T(8,128)(2,1)} collective-permute-done((bf16[2,128,1536]{2,1,0:T(8,128)(2,1)S(1)}, bf16[2,128,1536]{2,1,0:T(8,128)(2,1)}, u32[]{:S(2)}, u32[]{:S(2)}) %collective-permute-start.1) | collective-permute-done | bytes 786464 | tf_op jit(solution)/shard_map/ppermute | solution.py:14
  49.2 19.7 %collective-permute-done.2 = bf16[2,128,1536]{2,1,0:T(8,128)(2,1)} collective-permute-done((bf16[2,128,1536]{2,1,0:T(8,128)(2,1)}, bf16[2,128,1536]{2,1,0:T(8,128)(2,1)}, u32[]{:S(2)}, u32[]{:S(2)}) %collective-permute-start.2) | collective-permute-done | bytes 786464 | tf_op jit(solution)/shard_map/ppermute | solution.py:14
  74.1 5.4 %convolution_convert_fusion = bf16[1024,1152]{1,0:T(8,128)(2,1)} fusion(bf16[1024,1536]{1,0:T(8,128)(2,1)S(1)} %bitcast.63, bf16[1536,1152]{1,0:T(8,128)(2,1)S(1)} %copy-done), kind=kOutput, calls=%fused_computation.58 | convolution fusion | flops 3625058304 | bytes 9043968 | tf_op jit(solution)/shard_map/dot_general | solution.py:104
  79.5 4.6 %all-to-all-start = ((bf16[8,128,1152]{2,1,0:T(8,128)(2,1)}), bf16[8,128,1152]{2,1,0:T(8,128)(2,1)}, u32[]{:S(2)}, u32[]{:S(2)}) async-start(bf16[8,128,1152]{2,1,0:T(8,128)(2,1)} %bitcast.64), calls=%async_computation | async-start | bytes 4718592 | tf_op jit(solution)/shard_map/all_to_all | solution.py:110
  84.3 51.4 %all-to-all-done = bf16[8,128,1152]{2,1,0:T(8,128)(2,1)} async-done(((bf16[8,128,1152]{2,1,0:T(8,128)(2,1)}), bf16[8,128,1152]{2,1,0:T(8,128)(2,1)}, u32[]{:S(2)}, u32[]{:S(2)}) %all-to-all-start) | async-done | bytes 2359328 | tf_op jit(solution)/shard_map/all_to_all | solution.py:110
  135.7 4.3 %copy.20 = bf16[4,2,128,1152]{2,3,0,1:T(8,128)(2,1)} copy(bf16[4,2,128,1152]{3,2,1,0:T(8,128)(2,1)} %bitcast.2) | data formatting | bytes 4718592 | tf_op jit(solution)/shard_map/all_to_all | solution.py:110
  140.0 5.2 %fusion.56 = (bf16[2,1,4608]{1,2,0:T(8,128)(2,1)}, bf16[2,1,4608]{1,2,0:T(8,128)(2,1)}) fusion(bf16[2,128,4608]{1,2,0:T(8,128)(2,1)} %bitcast.60), kind=kLoop, calls=%fused_computation.120 | loop fusion | bytes 73728 | tf_op jit(solution)/shard_map/slice | solution.py:26
  145.3 2.7 copy.21
  149.9 2.7 copy.23
  152.6 3.6 %collective-permute-start.4 = (bf16[2,1,4608]{2,0,1:T(2,128)(2,1)}, bf16[2,1,4608]{2,0,1:T(2,128)(2,1)}, u32[]{:S(2)}, u32[]{:S(2)}) collective-permute-start(bf16[2,1,4608]{2,0,1:T(2,128)(2,1)} %copy.23), channel_id=1, source_target_pairs={{4,0},{8,4},{12,8},{5,1},{9,5},{13,9},{6,2},{10,6},{14,10},{7,3},{... | collective-permute-start | bytes 55304 | tf_op jit(solution)/shard_map/ppermute | solution.py:31
  158.0 2.6 copy.22
  160.6 2.7 copy.24
  163.3 7.6 %multiply_add_fusion = f32[2,128,4608]{1,2,0:T(8,128)S(1)} fusion(bf16[2,128,4608]{1,2,0:T(8,128)(2,1)} %bitcast.61, bf16[2,1,4608]{1,2,0:T(8,128)(2,1)} %copy.24, bf16[2,1,4608]{1,2,0:T(8,128)(2,1)} %copy.22, f32[4608]{0:T(1024)} %get-tuple-element.353, f32[4608]{0:T(1024)} %get-tuple-element.354, f32[4608]{0:T(1024)} %get-tuple-element.352), kind=kLoop, calls=%fused_computation.57 | loop fusion | flops 16515072 | bytes 7170048 | tf_op jit(solution)/shard_map/add | solution.py:113
  174.2 11.9 %all-gather = f32[4,1,384]{2,1,0:T(1,128)S(1)} all-gather(f32[1,1,384]{2,1,0:T(1,128)S(1)} %reshape.183), channel_id=1, replica_groups=mesh['groups'=2,'seq'=4,'fsdp'=4] {'fsdp'}, dimensions={0}, use_global_device_ids=true | all-gather | bytes 7680 | tf_op jit(solution)/shard_map/all_gather | solution.py:126
  189.0 18.5 %all_gather.9 = f32[2,64,1536]{2,1,0:T(8,128)} all-gather(f32[2,64,384]{2,1,0:T(8,128)} %param.19), channel_id=1, replica_groups=mesh['groups'=2,'seq'=4,'fsdp'=4] {'fsdp'}, dimensions={2}, use_global_device_ids=true | all-gather | bytes 983040 | tf_op jit(solution)/shard_map/all_gather | solution.py:125
  207.5 72.6 %while.16 = (s32[]{:T(128)}, f32[2,256,1536]{2,1,0:T(8,128)}, s32[]{:T(128)}, f32[17,64]{1,0:T(8,128)}, f32[64]{0:T(128)}, /*index=5*/f32[64,64]{1,0:T(8,128)}, ...) while((s32[]{:T(128)}, f32[2,256,1536]{2,1,0:T(8,128)}, ...), condition=%wide.region_1.2_spmd.clone, body=%wide.region_0.1_spmd.clone.sunk | while | flops 1934166400 | bytes 34141608 | solution.py:171
  211.6 2.6 convolution_bitcast_fusion.6
  215.5 2.7 convolution_bitcast_fusion.5
  220.7 4.3 %maximum_add_fusion.2 = f32[2,256,1536]{2,1,0:T(8,128)} fusion(f32[2,128,1536]{2,1,0:T(8,128)} %get-tuple-element.484, f32[2,128,1536]{2,1,0:T(8,128)} %get-tuple-element.485, f32[2,256,1536]{2,1,0:T(8,128)} %get-tuple-element.502, pred[]{:T(512)S(6)} %compare.8), kind=kLoop, calls=%fused_computation.2.clone.1 | loop fusion | flops 2359296 | bytes 9437185 | tf_op jit(solution)/shard_map/while/body/eval_jaxpr/add | solution.py:160
  229.0 2.6 convolution_bitcast_fusion.6
  232.9 2.7 convolution_bitcast_fusion.5
  235.6 2.5 select_subtract_fusion.2
  238.1 5.2 %maximum_add_fusion.2 = f32[2,256,1536]{2,1,0:T(8,128)} fusion(f32[2,128,1536]{2,1,0:T(8,128)} %get-tuple-element.484, f32[2,128,1536]{2,1,0:T(8,128)} %get-tuple-element.485, f32[2,256,1536]{2,1,0:T(8,128)} %get-tuple-element.502, pred[]{:T(512)S(6)} %compare.8), kind=kLoop, calls=%fused_computation.2.clone.1 | loop fusion | flops 2359296 | bytes 9437185 | tf_op jit(solution)/shard_map/while/body/eval_jaxpr/add | solution.py:160
  247.4 2.6 convolution_bitcast_fusion.6
  251.3 2.7 convolution_bitcast_fusion.5
  254.0 2.5 select_subtract_fusion.2
  256.5 5.2 %maximum_add_fusion.2 = f32[2,256,1536]{2,1,0:T(8,128)} fusion(f32[2,128,1536]{2,1,0:T(8,128)} %get-tuple-element.484, f32[2,128,1536]{2,1,0:T(8,128)} %get-tuple-element.485, f32[2,256,1536]{2,1,0:T(8,128)} %get-tuple-element.502, pred[]{:T(512)S(6)} %compare.8), kind=kLoop, calls=%fused_computation.2.clone.1 | loop fusion | flops 2359296 | bytes 9437185 | tf_op jit(solution)/shard_map/while/body/eval_jaxpr/add | solution.py:160
  265.8 2.6 convolution_bitcast_fusion.6
  269.7 2.7 convolution_bitcast_fusion.5
  274.9 5.2 %maximum_add_fusion.2 = f32[2,256,1536]{2,1,0:T(8,128)} fusion(f32[2,128,1536]{2,1,0:T(8,128)} %get-tuple-element.484, f32[2,128,1536]{2,1,0:T(8,128)} %get-tuple-element.485, f32[2,256,1536]{2,1,0:T(8,128)} %get-tuple-element.502, pred[]{:T(512)S(6)} %compare.8), kind=kLoop, calls=%fused_computation.2.clone.1 | loop fusion | flops 2359296 | bytes 9437185 | tf_op jit(solution)/shard_map/while/body/eval_jaxpr/add | solution.py:160
  280.1 8.8 %fusion.32 = bf16[2,128,1536]{1,2,0:T(8,128)(2,1)} fusion(f32[2,128,4608]{1,2,0:T(8,128)} %copy-done.3, f32[2,256,1536]{2,1,0:T(8,128)} %get-tuple-element.280, bf16[2,128,1536]{1,2,0:T(8,128)(2,1)} %fusion.31, f32[1536]{0:T(1024)S(1)} %reshape.184, f32[128,128]{1,0:T(8,128)} %get-tuple-element.392, f32[128,128]{1,0:T(8,128)} %get-tuple-element.391), kind=kOutput, calls=%fused_computation.67 | convolution fusion | flops 1209958400 | bytes 6428672 | tf_op jit(solution)/shard_map/if,sfd->sid/dot_general | solution.py:172
  (109 shorter events, 46.2 us)
Async XLA Ops:
  6.5 67.6 %copy-start = (bf16[1536,1152]{1,0:T(8,128)(2,1)S(1)}, bf16[1536,1152]{1,0:T(8,128)(2,1)}, u32[]{:S(2)}) copy-start(bf16[1536,1152]{1,0:T(8,128)(2,1)} %param.13) | copy-start | bytes 10616836
  6.5 21.4 %collective-permute-start = (bf16[2,128,1536]{2,1,0:T(8,128)(2,1)}, bf16[2,128,1536]{2,1,0:T(8,128)(2,1)S(1)}, u32[]{:S(2)}, u32[]{:S(2)}) collective-permute-start(bf16[2,128,1536]{2,1,0:T(8,128)(2,1)} %param.12), channel_id=1, source_target_pairs={{0,1},{1,2},{2,3},{3,0},{4,5},{5,6},{6,7},{7,4},{8,9},{9,10},{10,1... | collective-permute-start | bytes 2359304 | tf_op jit(solution)/shard_map/ppermute | solution.py:14
  27.9 0.9 copy-start.5
  28.8 20.4 %collective-permute-start.1 = (bf16[2,128,1536]{2,1,0:T(8,128)(2,1)S(1)}, bf16[2,128,1536]{2,1,0:T(8,128)(2,1)}, u32[]{:S(2)}, u32[]{:S(2)}) collective-permute-start(bf16[2,128,1536]{2,1,0:T(8,128)(2,1)S(1)} %collective-permute-done), channel_id=1, source_target_pairs={{0,1},{1,2},{2,3},{3,0},{4,5},{5,6},{6,7},{7,4},{8,9},{9,10},{10,1... | collective-permute-start | bytes 2359304 | tf_op jit(solution)/shard_map/ppermute | solution.py:14
  49.2 19.7 %collective-permute-start.2 = (bf16[2,128,1536]{2,1,0:T(8,128)(2,1)}, bf16[2,128,1536]{2,1,0:T(8,128)(2,1)}, u32[]{:S(2)}, u32[]{:S(2)}) collective-permute-start(bf16[2,128,1536]{2,1,0:T(8,128)(2,1)} %collective-permute-done.1), channel_id=1, source_target_pairs={{0,1},{1,2},{2,3},{3,0},{4,5},{5,6},{6,7},{7,4},{8,9},{9,10},{10,1... | collective-permute-start | bytes 2359304 | tf_op jit(solution)/shard_map/ppermute | solution.py:14
  49.2 22.0 %copy-start.6 = (bf16[2,128,1536]{2,1,0:T(8,128)(2,1)S(1)}, bf16[2,128,1536]{2,1,0:T(8,128)(2,1)}, u32[]{:S(2)}) copy-start(bf16[2,128,1536]{2,1,0:T(8,128)(2,1)} %copy-done.5) | copy-start | bytes 2359300
  49.2 22.1 %copy-start.4 = (bf16[2,128,1536]{2,1,0:T(8,128)(2,1)S(1)}, bf16[2,128,1536]{2,1,0:T(8,128)(2,1)}, u32[]{:S(2)}) copy-start(bf16[2,128,1536]{2,1,0:T(8,128)(2,1)} %param.12) | copy-start | bytes 2359300
  79.5 4.7 %copy-start.8 = (s32[2,1]{0,1:T(1,128)S(1)}, s32[2,1]{0,1:T(1,128)}, u32[]{:S(2)}) copy-start(s32[2,1]{0,1:T(1,128)} %param.21) | copy-start | bytes 28
  79.5 56.2 %all-to-all-start = ((bf16[8,128,1152]{2,1,0:T(8,128)(2,1)}), bf16[8,128,1152]{2,1,0:T(8,128)(2,1)}, u32[]{:S(2)}, u32[]{:S(2)}) async-start(bf16[8,128,1152]{2,1,0:T(8,128)(2,1)} %bitcast.64), calls=%async_computation | async-start | bytes 4718592 | tf_op jit(solution)/shard_map/all_to_all | solution.py:110
  84.2 123.3 %all-gather.3.cloned.1.call-start = ((), (), s32[]{:S(2)}) async-start(), calls=%async_computation.1 | async-start | bytes 3932160 | tf_op jit(solution)/shard_map/all_gather | solution.py:163
  148.0 10.0 %collective-permute-start.3 = (bf16[2,1,4608]{2,0,1:T(2,128)(2,1)}, bf16[2,1,4608]{2,0,1:T(2,128)(2,1)}, u32[]{:S(2)}, u32[]{:S(2)}) collective-permute-start(bf16[2,1,4608]{2,0,1:T(2,128)(2,1)} %copy.21), channel_id=1, source_target_pairs={{0,4},{4,8},{8,12},{1,5},{5,9},{9,13},{2,6},{6,10},{10,14},{3,7},{... | collective-permute-start | bytes 55304 | tf_op jit(solution)/shard_map/ppermute | solution.py:29
  152.6 8.1 %collective-permute-start.4 = (bf16[2,1,4608]{2,0,1:T(2,128)(2,1)}, bf16[2,1,4608]{2,0,1:T(2,128)(2,1)}, u32[]{:S(2)}, u32[]{:S(2)}) collective-permute-start(bf16[2,1,4608]{2,0,1:T(2,128)(2,1)} %copy.23), channel_id=1, source_target_pairs={{4,0},{8,4},{12,8},{5,1},{9,5},{13,9},{6,2},{10,6},{14,10},{7,3},{... | collective-permute-start | bytes 55304 | tf_op jit(solution)/shard_map/ppermute | solution.py:31
  170.9 2.1 copy-start.3
  173.0 1.1 copy-start.7
  215.5 2.7 copy-start.1
  215.5 2.7 copy-start.2
  232.9 2.7 copy-start.1
  232.9 2.7 copy-start.2
  251.3 2.7 copy-start.1
  251.3 2.7 copy-start.2
  269.7 2.7 copy-start.1
  269.7 2.7 copy-start.2
Sparse Core Ops, SparseCore 0:
  174.2 26.8 all-gather.2
